TPU v7x, 256 devices: a whole 4x4x8 slice. The times are simulated.
256 devices in a mesh: ctx: 16 (over z, core), head: 16 (over y, x).
Axes of the slice: x: 4, y: 4, z: 8, core: 2. Of those that a mesh axis runs over, the one named last changes fastest.
Arguments:
- x_proj: bfloat16 [8192, 8192], P('ctx', 'head'), may hold values from -6 to 6
- z_proj: bfloat16 [8192, 8192], P('ctx', 'head'), may hold values from -6 to 6
- b_proj: bfloat16 [8192, 128], P('ctx'), may hold values from -6 to 6
- c_proj: bfloat16 [8192, 128], P('ctx'), may hold values from -6 to 6
- dt_raw: float32 [128, 8192], P('head', 'ctx'), may hold values from -6 to -2
- a_log: float32 [128], P('head'), may hold values from -11 to 4
- d_skip: float32 [128], P('head'), may hold values from 0.5 to 2
- conv_x: float32 [4, 8192], P(None, 'head'), may hold values from -3 to 3
- conv_bc: float32 [4, 256], replicated, may hold values from -3 to 3
- norm_gain: float32 [8192], P('head'), may hold values from 0.5 to 1.5
- grad_out: bfloat16 [8192, 8192], P('ctx', 'head'), may hold values from -6 to 6
Outputs:
- y_out: bfloat16 [8192, 8192], P('ctx', 'head')
- grad_x: bfloat16 [8192, 8192], P('ctx', 'head')
- grad_z: bfloat16 [8192, 8192], P('ctx', 'head')
- grad_b: bfloat16 [8192, 128], P(('ctx', 'head'))
- grad_c: bfloat16 [8192, 128], P(('ctx', 'head'))
- grad_dt: float32 [128, 8192], P('head', 'ctx')
- grad_alog: float32 [128], P('head')
- grad_dskip: float32 [128], P('head')
- grad_convx: float32 [4, 8192], P(None, 'head')
- grad_convbc: float32 [4, 256], replicated
- grad_gain: float32 [8192], P('head')
All inputs are finite; a program needn't handle non-finite values.
Results may differ from a plain program's by a relative error of at most 0.023.
Values may be sent and summed in bfloat16 or wider, within the bound.
No kernel may reach another device: no remote copies, remote signals or barrier semaphores. Data moves between devices by JAX's collectives and lax.ppermute only.
A program may use at most 64 MiB of HBM per device.

v0:
```python
import jax
import jax.numpy as jnp
from jax import lax
from jax.sharding import PartitionSpec as P

HEADS = 128
HEAD_DIM = 64
GROUP = 256
HIGH = lax.Precision.HIGHEST
EPS = 1e-05


def passed_along(block, axis, distance):
    devices = range(lax.axis_size(axis))
    route = [(i - distance, i) for i in devices if i - distance in devices]
    return lax.ppermute(block, axis, route)


def silu_grad(value):
    sigma = jax.nn.sigmoid(value)
    return sigma * (1.0 + value * (1.0 - sigma))


def tap_sum(padded, weight, count):
    summed = jnp.zeros((count, padded.shape[1]), jnp.float32)
    for offset in range(weight.shape[0]):
        summed = summed + weight[offset][None, :] * padded[offset : offset + count].astype(
            jnp.float32
        )
    return summed


def back_taps(ahead, weight, count):
    final_tap = weight.shape[0] - 1
    summed = jnp.zeros((count, ahead.shape[1]), jnp.float32)
    for offset in range(weight.shape[0]):
        summed = (
            summed
            + weight[offset][None, :] * ahead[final_tap - offset : final_tap - offset + count]
        )
    return summed


def weight_taps(grad_pre, padded, count, tap_count):
    return jnp.stack(
        [
            jnp.sum(grad_pre * padded[offset : offset + count].astype(jnp.float32), axis=0)
            for offset in range(tap_count)
        ]
    )


def decay_table(cum_here):
    size_rows = cum_here.shape[0]
    row_ids = lax.broadcasted_iota(jnp.int32, (size_rows, size_rows), 0)
    col_ids = lax.broadcasted_iota(jnp.int32, (size_rows, size_rows), 1)
    allowed = (col_ids <= row_ids)[:, :, None]
    spread = cum_here[:, None, :] - cum_here[None, :, :]
    return jnp.where(allowed, jnp.exp(jnp.where(allowed, spread, 0.0)), 0.0)


def local(
    x_proj, z_proj, b_proj, c_proj, dt_raw, a_log, d_skip, conv_x, conv_bc, norm_gain, grad_out
):
    length = x_proj.shape[0]
    head_count = dt_raw.shape[0]
    row_width = x_proj.shape[1]
    head_dim = row_width // head_count
    state_dim = b_proj.shape[1]
    tap_count = conv_x.shape[0]
    blocks = length // GROUP
    channels = HEADS * HEAD_DIM
    bc_proj = jnp.concatenate([b_proj, c_proj], axis=1)
    edges = passed_along(
        (x_proj[length - tap_count + 1 :], bc_proj[length - tap_count + 1 :]), "ctx", 1
    )
    x_padded = jnp.concatenate([edges[0], x_proj], axis=0)
    bc_padded = jnp.concatenate([edges[1], bc_proj], axis=0)
    x_pre = tap_sum(x_padded, conv_x, length)
    bc_pre = tap_sum(bc_padded, conv_bc, length)
    x_act = jax.nn.silu(x_pre)
    bc_act = jax.nn.silu(bc_pre)
    decay_rate = jnp.exp(a_log)
    step_size = jax.nn.softplus(dt_raw).T
    x_blocks = x_act.reshape(blocks, GROUP, head_count, head_dim)
    b_blocks = bc_act[:, :state_dim].reshape(blocks, GROUP, state_dim)
    c_blocks = bc_act[:, state_dim:].reshape(blocks, GROUP, state_dim)
    d_blocks = step_size.reshape(blocks, GROUP, head_count)
    cum_blocks = jnp.cumsum(
        (-step_size * decay_rate[None, :]).reshape(blocks, GROUP, head_count), axis=1
    )
    block_ends = cum_blocks[:, -1, :]
    block_decay = jnp.exp(block_ends)
    tail_weight = jnp.exp(cum_blocks[:, -1:, :] - cum_blocks) * d_blocks
    block_states = jnp.einsum(
        "cshp,csn->chpn", tail_weight[..., None] * x_blocks, b_blocks, precision=HIGH
    )

    def fold_blocks(running, inputs):
        decay_now, state_now = inputs
        return (decay_now[:, None, None] * running + state_now, running)

    empty_state = jnp.zeros((head_count, head_dim, state_dim), jnp.float32)
    shard_state, local_entering = lax.scan(fold_blocks, empty_state, (block_decay, block_states))
    prefix_log = jnp.cumsum(block_ends, axis=0) - block_ends
    shard_decay = jnp.exp(jnp.sum(block_ends, axis=0))

    def pass_on(step_index, incoming):
        outgoing = shard_decay[:, None, None] * incoming + shard_state
        return passed_along(outgoing, "ctx", 1)

    entering = lax.fori_loop(0, lax.axis_size("ctx") - 1, pass_on, empty_state)
    block_entry = jnp.exp(prefix_log)[:, :, None, None] * entering[None] + local_entering

    def forward_block(inputs):
        x_here, b_here, c_here, d_here, cum_here, entry = inputs
        decay_map = decay_table(cum_here)
        scores = jnp.dot(c_here, b_here.T, precision=HIGH)
        mixing = scores[:, :, None] * decay_map * d_here[None, :, :]
        inside = jnp.einsum("tsh,shp->thp", mixing, x_here, precision=HIGH)
        carried = jnp.exp(cum_here)[:, :, None] * jnp.einsum(
            "tn,hpn->thp", c_here, entry, precision=HIGH
        )
        return inside + carried

    ssm_blocks = lax.map(
        forward_block, (x_blocks, b_blocks, c_blocks, d_blocks, cum_blocks, block_entry)
    )
    skip_rep = jnp.repeat(d_skip, head_dim)
    ssm_out = ssm_blocks.reshape(length, row_width) + skip_rep[None, :] * x_act
    z_float = z_proj.astype(jnp.float32)
    gate_act = jax.nn.silu(z_float)
    gated_out = ssm_out * gate_act
    grad_float = grad_out.astype(jnp.float32)
    scaled_grad = norm_gain[None, :] * grad_float
    square_sum, cross_sum = lax.psum(
        (jnp.sum(gated_out * gated_out, axis=1), jnp.sum(scaled_grad * gated_out, axis=1)), "head"
    )
    inv_rms = lax.rsqrt(square_sum / channels + EPS)[:, None]
    y_out = (gated_out * inv_rms * norm_gain[None, :]).astype(jnp.bfloat16)
    grad_gain_part = jnp.sum(grad_float * gated_out * inv_rms, axis=0)
    grad_gated = inv_rms * scaled_grad - gated_out * (inv_rms * inv_rms * inv_rms) * (
        cross_sum[:, None] / channels
    )
    grad_ssm = grad_gated * gate_act
    grad_z = (grad_gated * ssm_out * silu_grad(z_float)).astype(jnp.bfloat16)
    grad_skip_part = jnp.sum((grad_ssm * x_act).reshape(length, head_count, head_dim), axis=(0, 2))
    grad_blocks = grad_ssm.reshape(blocks, GROUP, head_count, head_dim)
    local_pull = jnp.einsum(
        "cthp,ctn->chpn", jnp.exp(cum_blocks)[..., None] * grad_blocks, c_blocks, precision=HIGH
    )
    shard_pull = jnp.sum(jnp.exp(prefix_log)[:, :, None, None] * local_pull, axis=0)

    def pass_back(step_index, incoming):
        outgoing = shard_decay[:, None, None] * incoming + shard_pull
        return passed_along(outgoing, "ctx", -1)

    leaving = lax.fori_loop(0, lax.axis_size("ctx") - 1, pass_back, empty_state)
    _, block_exit = lax.scan(fold_blocks, leaving, (block_decay, local_pull), reverse=True)

    def backward_block(inputs):
        x_here, b_here, c_here, d_here, cum_here, entry, exit_grad, grad_here = inputs
        decay_map = decay_table(cum_here)
        scores = jnp.dot(c_here, b_here.T, precision=HIGH)
        weighted = scores[:, :, None] * decay_map
        tail_decay = jnp.exp(cum_here[-1:, :] - cum_here)
        b_exit = jnp.einsum("sn,hpn->shp", b_here, exit_grad, precision=HIGH)
        pulled = (
            jnp.einsum("tsh,thp->shp", weighted, grad_here, precision=HIGH)
            + tail_decay[:, :, None] * b_exit
        )
        grad_x_here = d_here[:, :, None] * pulled
        grad_step = jnp.sum(x_here * pulled, axis=2)
        pair_grad = jnp.einsum("thp,shp->tsh", grad_here, x_here, precision=HIGH)
        masked = pair_grad * decay_map * d_here[None, :, :]
        grad_scores = jnp.sum(masked, axis=2)
        grad_c_here = jnp.dot(grad_scores, b_here, precision=HIGH)
        grad_b_here = jnp.dot(grad_scores.T, c_here, precision=HIGH)
        through = masked * scores[:, :, None]
        grad_cum = jnp.sum(through, axis=1) - jnp.sum(through, axis=0)
        start_map = jnp.exp(cum_here)[:, :, None] * grad_here
        carried = jnp.einsum("tn,hpn->thp", c_here, entry, precision=HIGH)
        grad_cum = grad_cum + jnp.sum(start_map * carried, axis=2)
        grad_c_here = grad_c_here + jnp.einsum("thp,hpn->tn", start_map, entry, precision=HIGH)
        release = tail_decay * d_here * jnp.sum(x_here * b_exit, axis=2)
        grad_cum = grad_cum - release
        end_total = jnp.sum(release, axis=0) + jnp.exp(cum_here[-1]) * jnp.sum(
            entry * exit_grad, axis=(1, 2)
        )
        grad_cum = jnp.concatenate([grad_cum[:-1], grad_cum[-1:] + end_total[None, :]], axis=0)
        grad_log = jnp.flip(jnp.cumsum(jnp.flip(grad_cum, 0), axis=0), 0)
        grad_b_here = grad_b_here + jnp.einsum(
            "shp,hpn->sn", (tail_decay * d_here)[:, :, None] * x_here, exit_grad, precision=HIGH
        )
        return (grad_x_here, grad_b_here, grad_c_here, grad_step, grad_log)

    grad_x_blocks, grad_b_blocks, grad_c_blocks, grad_step_blocks, grad_log_blocks = lax.map(
        backward_block,
        (x_blocks, b_blocks, c_blocks, d_blocks, cum_blocks, block_entry, block_exit, grad_blocks),
    )
    grad_log_rows = grad_log_blocks.reshape(length, head_count)
    grad_step_rows = (
        grad_step_blocks.reshape(length, head_count) - decay_rate[None, :] * grad_log_rows
    )
    grad_alog_part = decay_rate * -jnp.sum(step_size * grad_log_rows, axis=0)
    grad_dt = (grad_step_rows * jax.nn.sigmoid(dt_raw).T).T
    grad_x_act = grad_x_blocks.reshape(length, row_width) + skip_rep[None, :] * grad_ssm
    grad_bc_act = jnp.concatenate(
        [grad_b_blocks.reshape(length, state_dim), grad_c_blocks.reshape(length, state_dim)], axis=1
    )
    grad_x_pre = grad_x_act * silu_grad(x_pre)
    grad_bc_pre = grad_bc_act * silu_grad(bc_pre)
    ahead = passed_along((grad_x_pre[: tap_count - 1], grad_bc_pre[: tap_count - 1]), "ctx", -1)
    x_ahead = jnp.concatenate([grad_x_pre, ahead[0]], axis=0)
    bc_ahead = jnp.concatenate([grad_bc_pre, ahead[1]], axis=0)
    grad_x = back_taps(x_ahead, conv_x, length).astype(jnp.bfloat16)
    bc_back = back_taps(bc_ahead, conv_bc, length)
    shares = lax.psum_scatter(bc_back, "head", scatter_dimension=0, tiled=True)
    grad_b = shares[:, :state_dim].astype(jnp.bfloat16)
    grad_c = shares[:, state_dim:].astype(jnp.bfloat16)
    grad_convx_part = weight_taps(grad_x_pre, x_padded, length, tap_count)
    grad_convbc_part = weight_taps(grad_bc_pre, bc_padded, length, tap_count)
    grad_alog, grad_dskip, grad_convx, grad_gain = lax.psum(
        (grad_alog_part, grad_skip_part, grad_convx_part, grad_gain_part), "ctx"
    )
    grad_convbc = lax.psum(grad_convbc_part, ("ctx", "head"))
    return (
        y_out,
        grad_x,
        grad_z,
        grad_b,
        grad_c,
        grad_dt,
        grad_alog,
        grad_dskip,
        grad_convx,
        grad_convbc,
        grad_gain,
    )


def solution(mesh):
    return jax.shard_map(
        local,
        mesh=mesh,
        in_specs=(
            P("ctx", "head"),
            P("ctx", "head"),
            P("ctx", None),
            P("ctx", None),
            P("head", "ctx"),
            P("head"),
            P("head"),
            P(None, "head"),
            P(),
            P("head"),
            P("ctx", "head"),
        ),
        out_specs=(
            P("ctx", "head"),
            P("ctx", "head"),
            P("ctx", "head"),
            P(("ctx", "head"), None),
            P(("ctx", "head"), None),
            P("head", "ctx"),
            P("head"),
            P("head"),
            P(None, "head"),
            P(),
            P("head"),
        ),
        check_vma=False,
    )
```

profile of v0, /device:TPU:1, one launch (start us, length us, event | category | flops | bytes accessed | tf_op | source)
XLA Modules:
  0.0 672.7 jit_solution(3489720683614918270)
XLA Ops:
  8.2 4.9 collective-permute-start.2
  35.6 116.3 %while.77 = (s32[]{:T(128)}, f32[8,64,128]{2,1,0:T(8,128)S(1)}, f32[8]{0:T(128)S(1)}, f32[8,64,128]{2,1,0:T(8,128)S(1)}, s32[]{:T(128)}) while((s32[]{:T(128)}, f32[8,64,128]{2,1,0:T(8,128)S(1)}, f32[8]{0:T(128)S(1)}, f32[8,64,128]{2,1,0:T(8,128)S(1)}, s32[]{:T(128)}) %tuple.173), condition=%wide.region_7.8_spmd, body=%wide.region_6.7_spmd.sunk | while | flops 131074 | bytes 1835141 | solution.py:112
  43.0 4.4 collective-permute-start
  50.8 4.4 collective-permute-start
  153.4 36.2 %while.78 = (s32[]{:T(128)}, f32[2,256,8,64]{1,0,3,2:T(2,128)}, f32[2,256,8,64]{1,3,2,0:T(8,128)}, f32[2,256,128]{2,1,0:T(8,128)S(1)}, f32[2,256,128]{2,1,0:T(8,...) while((s32[]{:T(128)}, f32[2,256,8,64]{1,0,3,2:T(2,128)}, ...), condition=%wide.region_9.10_spmd, body=%wide.region_8.9_spmd.sunk | while | flops 707592192 | bytes 5580925 | solution.py:126
  160.0 11.5 %dynamic_update_slice.48 = f32[2,256,8,64]{1,0,3,2:T(2,128)} dynamic-update-slice(f32[2,256,8,64]{1,0,3,2:T(2,128)} %get-tuple-element.953, f32[1,256,8,64]{1,0,3,2:T(1,128)S(1)} %copy.218, s32[]{:T(128)S(6)} %copy.254, s32[]{:T(128)} %constant.125.clone.1..sunk, s32[]{:T(128)} %constant.125.clone.1..sunk, s32[]{:T(128)} %constant.125.clone.1..sunk) | dynamic-update-slice | bytes 1048580 | tf_op jit(solution)/shard_map/while/body/jit(dynamic_update_index_in_dim)/dynamic_update_slice | solution.py:126
  178.1 11.5 %dynamic_update_slice.48 = f32[2,256,8,64]{1,0,3,2:T(2,128)} dynamic-update-slice(f32[2,256,8,64]{1,0,3,2:T(2,128)} %get-tuple-element.953, f32[1,256,8,64]{1,0,3,2:T(1,128)S(1)} %copy.218, s32[]{:T(128)S(6)} %copy.254, s32[]{:T(128)} %constant.125.clone.1..sunk, s32[]{:T(128)} %constant.125.clone.1..sunk, s32[]{:T(128)} %constant.125.clone.1..sunk) | dynamic-update-slice | bytes 1048580 | tf_op jit(solution)/shard_map/while/body/jit(dynamic_update_index_in_dim)/dynamic_update_slice | solution.py:126
  192.0 33.5 %psum.49 = f32[512]{0:T(512)S(1)} all-reduce(f32[512]{0:T(512)S(1)} %get-tuple-element.601), channel_id=1, replica_groups=mesh['ctx'=16,'head'=16] {'head'}, use_global_device_ids=true, to_apply=%region_11.12 | all-reduce | flops 512 | bytes 4096 | tf_op jit(solution)/shard_map/psum | solution.py:136
  227.5 28.9 %psum.50 = f32[512]{0:T(512)S(1)} all-reduce(f32[512]{0:T(512)S(1)} %get-tuple-element.496), channel_id=1, replica_groups=mesh['ctx'=16,'head'=16] {'head'}, use_global_device_ids=true, to_apply=%region_13.14 | all-reduce | flops 512 | bytes 4096 | tf_op jit(solution)/shard_map/psum | solution.py:136
  256.4 4.5 multiply_reduce_fusion.3
  263.5 146.2 %while.79 = (s32[]{:T(128)}, f32[8,64,128]{2,1,0:T(8,128)S(1)}, f32[8]{0:T(128)S(1)}, f32[8,64,128]{2,1,0:T(8,128)S(1)}, s32[]{:T(128)}) while((s32[]{:T(128)}, f32[8,64,128]{2,1,0:T(8,128)S(1)}, f32[8]{0:T(128)S(1)}, f32[8,64,128]{2,1,0:T(8,128)S(1)}, s32[]{:T(128)}) %tuple.195), condition=%wide.region_16.17_spmd, body=%wide.region_15.16_spmd.sunk | while | flops 131074 | bytes 1835141 | solution.py:158
  263.6 11.7 %collective-permute-start.1 = (f32[8,64,128]{2,1,0:T(8,128)S(1)}, f32[8,64,128]{2,1,0:T(8,128)S(1)}, u32[]{:S(2)}, u32[]{:S(2)}) collective-permute-start(f32[8,64,128]{2,1,0:T(8,128)S(1)} %multiply_add_fusion.7), channel_id=1, source_target_pairs={{16,0},{32,16},{48,32},{64,48},{80,64},{96,80},{112,96},{128,112},... | collective-permute-start | bytes 786440 | tf_op jit(solution)/shard_map/while/body/eval_jaxpr/ppermute | solution.py:16
  275.3 10.6 %collective-permute-done.1 = f32[8,64,128]{2,1,0:T(8,128)S(1)} collective-permute-done((f32[8,64,128]{2,1,0:T(8,128)S(1)}, f32[8,64,128]{2,1,0:T(8,128)S(1)}, u32[]{:S(2)}, u32[]{:S(2)}) %collective-permute-start.1) | collective-permute-done | bytes 262176 | tf_op jit(solution)/shard_map/while/body/eval_jaxpr/ppermute | solution.py:16
  287.9 5.8 collective-permute-done.1
  295.7 5.8 collective-permute-done.1
  303.5 5.8 collective-permute-done.1
  311.3 7.8 %collective-permute-done.1 = f32[8,64,128]{2,1,0:T(8,128)S(1)} collective-permute-done((f32[8,64,128]{2,1,0:T(8,128)S(1)}, f32[8,64,128]{2,1,0:T(8,128)S(1)}, u32[]{:S(2)}, u32[]{:S(2)}) %collective-permute-start.1) | collective-permute-done | bytes 262176 | tf_op jit(solution)/shard_map/while/body/eval_jaxpr/ppermute | solution.py:16
  321.1 5.8 collective-permute-done.1
  328.9 8.8 %collective-permute-done.1 = f32[8,64,128]{2,1,0:T(8,128)S(1)} collective-permute-done((f32[8,64,128]{2,1,0:T(8,128)S(1)}, f32[8,64,128]{2,1,0:T(8,128)S(1)}, u32[]{:S(2)}, u32[]{:S(2)}) %collective-permute-start.1) | collective-permute-done | bytes 262176 | tf_op jit(solution)/shard_map/while/body/eval_jaxpr/ppermute | solution.py:16
  339.7 7.0 %collective-permute-done.1 = f32[8,64,128]{2,1,0:T(8,128)S(1)} collective-permute-done((f32[8,64,128]{2,1,0:T(8,128)S(1)}, f32[8,64,128]{2,1,0:T(8,128)S(1)}, u32[]{:S(2)}, u32[]{:S(2)}) %collective-permute-start.1) | collective-permute-done | bytes 262176 | tf_op jit(solution)/shard_map/while/body/eval_jaxpr/ppermute | solution.py:16
  348.7 7.0 %collective-permute-done.1 = f32[8,64,128]{2,1,0:T(8,128)S(1)} collective-permute-done((f32[8,64,128]{2,1,0:T(8,128)S(1)}, f32[8,64,128]{2,1,0:T(8,128)S(1)}, u32[]{:S(2)}, u32[]{:S(2)}) %collective-permute-start.1) | collective-permute-done | bytes 262176 | tf_op jit(solution)/shard_map/while/body/eval_jaxpr/ppermute | solution.py:16
  357.7 7.0 %collective-permute-done.1 = f32[8,64,128]{2,1,0:T(8,128)S(1)} collective-permute-done((f32[8,64,128]{2,1,0:T(8,128)S(1)}, f32[8,64,128]{2,1,0:T(8,128)S(1)}, u32[]{:S(2)}, u32[]{:S(2)}) %collective-permute-start.1) | collective-permute-done | bytes 262176 | tf_op jit(solution)/shard_map/while/body/eval_jaxpr/ppermute | solution.py:16
  366.7 7.0 %collective-permute-done.1 = f32[8,64,128]{2,1,0:T(8,128)S(1)} collective-permute-done((f32[8,64,128]{2,1,0:T(8,128)S(1)}, f32[8,64,128]{2,1,0:T(8,128)S(1)}, u32[]{:S(2)}, u32[]{:S(2)}) %collective-permute-start.1) | collective-permute-done | bytes 262176 | tf_op jit(solution)/shard_map/while/body/eval_jaxpr/ppermute | solution.py:16
  375.7 7.0 %collective-permute-done.1 = f32[8,64,128]{2,1,0:T(8,128)S(1)} collective-permute-done((f32[8,64,128]{2,1,0:T(8,128)S(1)}, f32[8,64,128]{2,1,0:T(8,128)S(1)}, u32[]{:S(2)}, u32[]{:S(2)}) %collective-permute-start.1) | collective-permute-done | bytes 262176 | tf_op jit(solution)/shard_map/while/body/eval_jaxpr/ppermute | solution.py:16
  384.7 7.0 %collective-permute-done.1 = f32[8,64,128]{2,1,0:T(8,128)S(1)} collective-permute-done((f32[8,64,128]{2,1,0:T(8,128)S(1)}, f32[8,64,128]{2,1,0:T(8,128)S(1)}, u32[]{:S(2)}, u32[]{:S(2)}) %collective-permute-start.1) | collective-permute-done | bytes 262176 | tf_op jit(solution)/shard_map/while/body/eval_jaxpr/ppermute | solution.py:16
  393.7 7.0 %collective-permute-done.1 = f32[8,64,128]{2,1,0:T(8,128)S(1)} collective-permute-done((f32[8,64,128]{2,1,0:T(8,128)S(1)}, f32[8,64,128]{2,1,0:T(8,128)S(1)}, u32[]{:S(2)}, u32[]{:S(2)}) %collective-permute-start.1) | collective-permute-done | bytes 262176 | tf_op jit(solution)/shard_map/while/body/eval_jaxpr/ppermute | solution.py:16
  402.7 7.0 %collective-permute-done.1 = f32[8,64,128]{2,1,0:T(8,128)S(1)} collective-permute-done((f32[8,64,128]{2,1,0:T(8,128)S(1)}, f32[8,64,128]{2,1,0:T(8,128)S(1)}, u32[]{:S(2)}, u32[]{:S(2)}) %collective-permute-start.1) | collective-permute-done | bytes 262176 | tf_op jit(solution)/shard_map/while/body/eval_jaxpr/ppermute | solution.py:16
  411.4 87.2 %while.81 = (s32[]{:T(128)}, f32[2,256,8,64]{1,0,3,2:T(2,128)}, f32[2,256,128]{2,1,0:T(8,128)}, f32[2,256,128]{2,1,0:T(8,128)}, f32[2,256,8]{1,2,0:T(8,128)}, /*...) while((s32[]{:T(128)}, f32[2,256,8,64]{1,0,3,2:T(2,128)}, ...), condition=%wide.region_30.31_spmd, body=%wide.region_19.30_spmd.sunk | while | flops 1921460224 | bytes 14728557 | solution.py:197
  443.5 11.5 %dynamic_update_slice.53 = f32[2,256,8,64]{1,0,3,2:T(2,128)} dynamic-update-slice(f32[2,256,8,64]{1,0,3,2:T(2,128)} %get-tuple-element.1024, f32[1,256,8,64]{1,0,3,2:T(1,128)S(1)} %copy.224, s32[]{:T(128)S(6)} %copy.279, s32[]{:T(128)} %constant.125.clone.1..sunk.1, s32[]{:T(128)} %constant.125.clone.1..sunk.1, s32[]{:T(128)} %constant.125.clone.1..sunk.1) | dynamic-update-slice | bytes 1048580 | tf_op jit(solution)/shard_map/while/body/jit(dynamic_update_index_in_dim)/dynamic_update_slice | solution.py:126
  487.1 11.5 %dynamic_update_slice.53 = f32[2,256,8,64]{1,0,3,2:T(2,128)} dynamic-update-slice(f32[2,256,8,64]{1,0,3,2:T(2,128)} %get-tuple-element.1024, f32[1,256,8,64]{1,0,3,2:T(1,128)S(1)} %copy.224, s32[]{:T(128)S(6)} %copy.279, s32[]{:T(128)} %constant.125.clone.1..sunk.1, s32[]{:T(128)} %constant.125.clone.1..sunk.1, s32[]{:T(128)} %constant.125.clone.1..sunk.1) | dynamic-update-slice | bytes 1048580 | tf_op jit(solution)/shard_map/while/body/jit(dynamic_update_index_in_dim)/dynamic_update_slice | solution.py:126
  515.5 62.7 %all-reduce = (f32[8]{0:T(128)}, f32[8]{0:T(128)}, f32[4,512]{1,0:T(4,128)}, f32[512]{0:T(512)}) all-reduce(f32[8]{0:T(128)S(1)} %negate_multiply_fusion, f32[8]{0:T(128)S(1)} %reduce_sum.225, f32[4,512]{1,0:T(4,128)S(1)} %pad_maximum_fusion.5, f32[512]{0:T(512)S(1)} %copy-done.40), channel_id=1, replica_groups=mesh['ctx'=16,'head'=16] {'ctx'}, use_global_device_ids=true, to_apply=%region_33.34 | all-reduce | flops 2576 | bytes 20608 | tf_op jit(solution)/shard_map/psum | solution.py:223
  581.2 80.8 %psum.54 = f32[4,256]{1,0:T(4,128)} all-reduce(f32[4,256]{1,0:T(4,128)S(1)} %pad_maximum_fusion.6), channel_id=1, replica_groups=mesh['ctx'=16,'head'=16] {'ctx','head'}, use_global_device_ids=true, to_apply=%region_46.47 | all-reduce | flops 1024 | bytes 8192 | tf_op jit(solution)/shard_map/psum | solution.py:226
  (340 shorter events, 269.9 us)
Async XLA Ops:
  7.2 657.3 %reduce-scatter.2.cloned.1.call-start = ((), (), s32[]{:S(2)}) async-start(), calls=%async_computation.1 | async-start | bytes 557056 | tf_op jit(solution)/shard_map/reduce_scatter | solution.py:218
  8.2 20.1 %collective-permute-start.2 = (bf16[3,512]{0,1:T(8,128)(2,1)S(1)}, bf16[3,512]{0,1:T(8,128)(2,1)S(1)}, u32[]{:S(2)}, u32[]{:S(2)}) collective-permute-start(bf16[3,512]{0,1:T(8,128)(2,1)S(1)} %copy.135), channel_id=1, source_target_pairs={{0,16},{16,32},{32,48},{48,64},{64,80},{80,96},{96,112},{112,128},... | collective-permute-start | bytes 9224 | tf_op jit(solution)/shard_map/ppermute | solution.py:16
  15.0 12.9 %collective-permute-start.3 = (bf16[3,256]{1,0:T(4,128)(2,1)S(1)}, bf16[3,256]{1,0:T(4,128)(2,1)S(1)}, u32[]{:S(2)}, u32[]{:S(2)}) collective-permute-start(bf16[3,256]{1,0:T(4,128)(2,1)S(1)} %slice.165), channel_id=1, source_target_pairs={{0,16},{16,32},{32,48},{48,64},{64,80},{80,96},{96,112},{112,128},... | collective-permute-start | bytes 4616 | tf_op jit(solution)/shard_map/ppermute | solution.py:16
  43.0 7.7 %collective-permute-start = (f32[8,64,128]{2,1,0:T(8,128)S(1)}, f32[8,64,128]{2,1,0:T(8,128)S(1)}, u32[]{:S(2)}, u32[]{:S(2)}) collective-permute-start(f32[8,64,128]{2,1,0:T(8,128)S(1)} %multiply_add_fusion.6), channel_id=1, source_target_pairs={{0,16},{16,32},{32,48},{48,64},{64,80},{80,96},{96,112},{112,128},... | collective-permute-start | bytes 786440 | tf_op jit(solution)/shard_map/while/body/eval_jaxpr/ppermute | solution.py:16
  50.8 7.7 %collective-permute-start = (f32[8,64,128]{2,1,0:T(8,128)S(1)}, f32[8,64,128]{2,1,0:T(8,128)S(1)}, u32[]{:S(2)}, u32[]{:S(2)}) collective-permute-start(f32[8,64,128]{2,1,0:T(8,128)S(1)} %multiply_add_fusion.6), channel_id=1, source_target_pairs={{0,16},{16,32},{32,48},{48,64},{64,80},{80,96},{96,112},{112,128},... | collective-permute-start | bytes 786440 | tf_op jit(solution)/shard_map/while/body/eval_jaxpr/ppermute | solution.py:16
  58.6 7.7 %collective-permute-start = (f32[8,64,128]{2,1,0:T(8,128)S(1)}, f32[8,64,128]{2,1,0:T(8,128)S(1)}, u32[]{:S(2)}, u32[]{:S(2)}) collective-permute-start(f32[8,64,128]{2,1,0:T(8,128)S(1)} %multiply_add_fusion.6), channel_id=1, source_target_pairs={{0,16},{16,32},{32,48},{48,64},{64,80},{80,96},{96,112},{112,128},... | collective-permute-start | bytes 786440 | tf_op jit(solution)/shard_map/while/body/eval_jaxpr/ppermute | solution.py:16
  66.4 7.7 %collective-permute-start = (f32[8,64,128]{2,1,0:T(8,128)S(1)}, f32[8,64,128]{2,1,0:T(8,128)S(1)}, u32[]{:S(2)}, u32[]{:S(2)}) collective-permute-start(f32[8,64,128]{2,1,0:T(8,128)S(1)} %multiply_add_fusion.6), channel_id=1, source_target_pairs={{0,16},{16,32},{32,48},{48,64},{64,80},{80,96},{96,112},{112,128},... | collective-permute-start | bytes 786440 | tf_op jit(solution)/shard_map/while/body/eval_jaxpr/ppermute | solution.py:16
  74.2 7.7 %collective-permute-start = (f32[8,64,128]{2,1,0:T(8,128)S(1)}, f32[8,64,128]{2,1,0:T(8,128)S(1)}, u32[]{:S(2)}, u32[]{:S(2)}) collective-permute-start(f32[8,64,128]{2,1,0:T(8,128)S(1)} %multiply_add_fusion.6), channel_id=1, source_target_pairs={{0,16},{16,32},{32,48},{48,64},{64,80},{80,96},{96,112},{112,128},... | collective-permute-start | bytes 786440 | tf_op jit(solution)/shard_map/while/body/eval_jaxpr/ppermute | solution.py:16
  82.0 7.7 %collective-permute-start = (f32[8,64,128]{2,1,0:T(8,128)S(1)}, f32[8,64,128]{2,1,0:T(8,128)S(1)}, u32[]{:S(2)}, u32[]{:S(2)}) collective-permute-start(f32[8,64,128]{2,1,0:T(8,128)S(1)} %multiply_add_fusion.6), channel_id=1, source_target_pairs={{0,16},{16,32},{32,48},{48,64},{64,80},{80,96},{96,112},{112,128},... | collective-permute-start | bytes 786440 | tf_op jit(solution)/shard_map/while/body/eval_jaxpr/ppermute | solution.py:16
  89.8 7.7 %collective-permute-start = (f32[8,64,128]{2,1,0:T(8,128)S(1)}, f32[8,64,128]{2,1,0:T(8,128)S(1)}, u32[]{:S(2)}, u32[]{:S(2)}) collective-permute-start(f32[8,64,128]{2,1,0:T(8,128)S(1)} %multiply_add_fusion.6), channel_id=1, source_target_pairs={{0,16},{16,32},{32,48},{48,64},{64,80},{80,96},{96,112},{112,128},... | collective-permute-start | bytes 786440 | tf_op jit(solution)/shard_map/while/body/eval_jaxpr/ppermute | solution.py:16
  97.5 7.7 %collective-permute-start = (f32[8,64,128]{2,1,0:T(8,128)S(1)}, f32[8,64,128]{2,1,0:T(8,128)S(1)}, u32[]{:S(2)}, u32[]{:S(2)}) collective-permute-start(f32[8,64,128]{2,1,0:T(8,128)S(1)} %multiply_add_fusion.6), channel_id=1, source_target_pairs={{0,16},{16,32},{32,48},{48,64},{64,80},{80,96},{96,112},{112,128},... | collective-permute-start | bytes 786440 | tf_op jit(solution)/shard_map/while/body/eval_jaxpr/ppermute | solution.py:16
  105.3 7.7 %collective-permute-start = (f32[8,64,128]{2,1,0:T(8,128)S(1)}, f32[8,64,128]{2,1,0:T(8,128)S(1)}, u32[]{:S(2)}, u32[]{:S(2)}) collective-permute-start(f32[8,64,128]{2,1,0:T(8,128)S(1)} %multiply_add_fusion.6), channel_id=1, source_target_pairs={{0,16},{16,32},{32,48},{48,64},{64,80},{80,96},{96,112},{112,128},... | collective-permute-start | bytes 786440 | tf_op jit(solution)/shard_map/while/body/eval_jaxpr/ppermute | solution.py:16
  113.1 7.7 %collective-permute-start = (f32[8,64,128]{2,1,0:T(8,128)S(1)}, f32[8,64,128]{2,1,0:T(8,128)S(1)}, u32[]{:S(2)}, u32[]{:S(2)}) collective-permute-start(f32[8,64,128]{2,1,0:T(8,128)S(1)} %multiply_add_fusion.6), channel_id=1, source_target_pairs={{0,16},{16,32},{32,48},{48,64},{64,80},{80,96},{96,112},{112,128},... | collective-permute-start | bytes 786440 | tf_op jit(solution)/shard_map/while/body/eval_jaxpr/ppermute | solution.py:16
  120.9 7.7 %collective-permute-start = (f32[8,64,128]{2,1,0:T(8,128)S(1)}, f32[8,64,128]{2,1,0:T(8,128)S(1)}, u32[]{:S(2)}, u32[]{:S(2)}) collective-permute-start(f32[8,64,128]{2,1,0:T(8,128)S(1)} %multiply_add_fusion.6), channel_id=1, source_target_pairs={{0,16},{16,32},{32,48},{48,64},{64,80},{80,96},{96,112},{112,128},... | collective-permute-start | bytes 786440 | tf_op jit(solution)/shard_map/while/body/eval_jaxpr/ppermute | solution.py:16
  128.7 7.7 %collective-permute-start = (f32[8,64,128]{2,1,0:T(8,128)S(1)}, f32[8,64,128]{2,1,0:T(8,128)S(1)}, u32[]{:S(2)}, u32[]{:S(2)}) collective-permute-start(f32[8,64,128]{2,1,0:T(8,128)S(1)} %multiply_add_fusion.6), channel_id=1, source_target_pairs={{0,16},{16,32},{32,48},{48,64},{64,80},{80,96},{96,112},{112,128},... | collective-permute-start | bytes 786440 | tf_op jit(solution)/shard_map/while/body/eval_jaxpr/ppermute | solution.py:16
  136.5 7.7 %collective-permute-start = (f32[8,64,128]{2,1,0:T(8,128)S(1)}, f32[8,64,128]{2,1,0:T(8,128)S(1)}, u32[]{:S(2)}, u32[]{:S(2)}) collective-permute-start(f32[8,64,128]{2,1,0:T(8,128)S(1)} %multiply_add_fusion.6), channel_id=1, source_target_pairs={{0,16},{16,32},{32,48},{48,64},{64,80},{80,96},{96,112},{112,128},... | collective-permute-start | bytes 786440 | tf_op jit(solution)/shard_map/while/body/eval_jaxpr/ppermute | solution.py:16
  144.3 7.7 %collective-permute-start = (f32[8,64,128]{2,1,0:T(8,128)S(1)}, f32[8,64,128]{2,1,0:T(8,128)S(1)}, u32[]{:S(2)}, u32[]{:S(2)}) collective-permute-start(f32[8,64,128]{2,1,0:T(8,128)S(1)} %multiply_add_fusion.6), channel_id=1, source_target_pairs={{0,16},{16,32},{32,48},{48,64},{64,80},{80,96},{96,112},{112,128},... | collective-permute-start | bytes 786440 | tf_op jit(solution)/shard_map/while/body/eval_jaxpr/ppermute | solution.py:16
  263.6 22.3 %collective-permute-start.1 = (f32[8,64,128]{2,1,0:T(8,128)S(1)}, f32[8,64,128]{2,1,0:T(8,128)S(1)}, u32[]{:S(2)}, u32[]{:S(2)}) collective-permute-start(f32[8,64,128]{2,1,0:T(8,128)S(1)} %multiply_add_fusion.7), channel_id=1, source_target_pairs={{16,0},{32,16},{48,32},{64,48},{80,64},{96,80},{112,96},{128,112},... | collective-permute-start | bytes 786440 | tf_op jit(solution)/shard_map/while/body/eval_jaxpr/ppermute | solution.py:16
  293.8 7.7 %collective-permute-start.1 = (f32[8,64,128]{2,1,0:T(8,128)S(1)}, f32[8,64,128]{2,1,0:T(8,128)S(1)}, u32[]{:S(2)}, u32[]{:S(2)}) collective-permute-start(f32[8,64,128]{2,1,0:T(8,128)S(1)} %multiply_add_fusion.7), channel_id=1, source_target_pairs={{16,0},{32,16},{48,32},{64,48},{80,64},{96,80},{112,96},{128,112},... | collective-permute-start | bytes 786440 | tf_op jit(solution)/shard_map/while/body/eval_jaxpr/ppermute | solution.py:16
  301.6 7.7 %collective-permute-start.1 = (f32[8,64,128]{2,1,0:T(8,128)S(1)}, f32[8,64,128]{2,1,0:T(8,128)S(1)}, u32[]{:S(2)}, u32[]{:S(2)}) collective-permute-start(f32[8,64,128]{2,1,0:T(8,128)S(1)} %multiply_add_fusion.7), channel_id=1, source_target_pairs={{16,0},{32,16},{48,32},{64,48},{80,64},{96,80},{112,96},{128,112},... | collective-permute-start | bytes 786440 | tf_op jit(solution)/shard_map/while/body/eval_jaxpr/ppermute | solution.py:16
  309.3 9.7 %collective-permute-start.1 = (f32[8,64,128]{2,1,0:T(8,128)S(1)}, f32[8,64,128]{2,1,0:T(8,128)S(1)}, u32[]{:S(2)}, u32[]{:S(2)}) collective-permute-start(f32[8,64,128]{2,1,0:T(8,128)S(1)} %multiply_add_fusion.7), channel_id=1, source_target_pairs={{16,0},{32,16},{48,32},{64,48},{80,64},{96,80},{112,96},{128,112},... | collective-permute-start | bytes 786440 | tf_op jit(solution)/shard_map/while/body/eval_jaxpr/ppermute | solution.py:16
  319.2 7.7 %collective-permute-start.1 = (f32[8,64,128]{2,1,0:T(8,128)S(1)}, f32[8,64,128]{2,1,0:T(8,128)S(1)}, u32[]{:S(2)}, u32[]{:S(2)}) collective-permute-start(f32[8,64,128]{2,1,0:T(8,128)S(1)} %multiply_add_fusion.7), channel_id=1, source_target_pairs={{16,0},{32,16},{48,32},{64,48},{80,64},{96,80},{112,96},{128,112},... | collective-permute-start | bytes 786440 | tf_op jit(solution)/shard_map/while/body/eval_jaxpr/ppermute | solution.py:16
  327.0 10.7 %collective-permute-start.1 = (f32[8,64,128]{2,1,0:T(8,128)S(1)}, f32[8,64,128]{2,1,0:T(8,128)S(1)}, u32[]{:S(2)}, u32[]{:S(2)}) collective-permute-start(f32[8,64,128]{2,1,0:T(8,128)S(1)} %multiply_add_fusion.7), channel_id=1, source_target_pairs={{16,0},{32,16},{48,32},{64,48},{80,64},{96,80},{112,96},{128,112},... | collective-permute-start | bytes 786440 | tf_op jit(solution)/shard_map/while/body/eval_jaxpr/ppermute | solution.py:16
  337.8 8.9 %collective-permute-start.1 = (f32[8,64,128]{2,1,0:T(8,128)S(1)}, f32[8,64,128]{2,1,0:T(8,128)S(1)}, u32[]{:S(2)}, u32[]{:S(2)}) collective-permute-start(f32[8,64,128]{2,1,0:T(8,128)S(1)} %multiply_add_fusion.7), channel_id=1, source_target_pairs={{16,0},{32,16},{48,32},{64,48},{80,64},{96,80},{112,96},{128,112},... | collective-permute-start | bytes 786440 | tf_op jit(solution)/shard_map/while/body/eval_jaxpr/ppermute | solution.py:16
  346.8 8.9 %collective-permute-start.1 = (f32[8,64,128]{2,1,0:T(8,128)S(1)}, f32[8,64,128]{2,1,0:T(8,128)S(1)}, u32[]{:S(2)}, u32[]{:S(2)}) collective-permute-start(f32[8,64,128]{2,1,0:T(8,128)S(1)} %multiply_add_fusion.7), channel_id=1, source_target_pairs={{16,0},{32,16},{48,32},{64,48},{80,64},{96,80},{112,96},{128,112},... | collective-permute-start | bytes 786440 | tf_op jit(solution)/shard_map/while/body/eval_jaxpr/ppermute | solution.py:16
  355.8 8.9 %collective-permute-start.1 = (f32[8,64,128]{2,1,0:T(8,128)S(1)}, f32[8,64,128]{2,1,0:T(8,128)S(1)}, u32[]{:S(2)}, u32[]{:S(2)}) collective-permute-start(f32[8,64,128]{2,1,0:T(8,128)S(1)} %multiply_add_fusion.7), channel_id=1, source_target_pairs={{16,0},{32,16},{48,32},{64,48},{80,64},{96,80},{112,96},{128,112},... | collective-permute-start | bytes 786440 | tf_op jit(solution)/shard_map/while/body/eval_jaxpr/ppermute | solution.py:16
  364.8 8.9 %collective-permute-start.1 = (f32[8,64,128]{2,1,0:T(8,128)S(1)}, f32[8,64,128]{2,1,0:T(8,128)S(1)}, u32[]{:S(2)}, u32[]{:S(2)}) collective-permute-start(f32[8,64,128]{2,1,0:T(8,128)S(1)} %multiply_add_fusion.7), channel_id=1, source_target_pairs={{16,0},{32,16},{48,32},{64,48},{80,64},{96,80},{112,96},{128,112},... | collective-permute-start | bytes 786440 | tf_op jit(solution)/shard_map/while/body/eval_jaxpr/ppermute | solution.py:16
  373.8 8.9 %collective-permute-start.1 = (f32[8,64,128]{2,1,0:T(8,128)S(1)}, f32[8,64,128]{2,1,0:T(8,128)S(1)}, u32[]{:S(2)}, u32[]{:S(2)}) collective-permute-start(f32[8,64,128]{2,1,0:T(8,128)S(1)} %multiply_add_fusion.7), channel_id=1, source_target_pairs={{16,0},{32,16},{48,32},{64,48},{80,64},{96,80},{112,96},{128,112},... | collective-permute-start | bytes 786440 | tf_op jit(solution)/shard_map/while/body/eval_jaxpr/ppermute | solution.py:16
  382.8 8.9 %collective-permute-start.1 = (f32[8,64,128]{2,1,0:T(8,128)S(1)}, f32[8,64,128]{2,1,0:T(8,128)S(1)}, u32[]{:S(2)}, u32[]{:S(2)}) collective-permute-start(f32[8,64,128]{2,1,0:T(8,128)S(1)} %multiply_add_fusion.7), channel_id=1, source_target_pairs={{16,0},{32,16},{48,32},{64,48},{80,64},{96,80},{112,96},{128,112},... | collective-permute-start | bytes 786440 | tf_op jit(solution)/shard_map/while/body/eval_jaxpr/ppermute | solution.py:16
  391.8 8.9 %collective-permute-start.1 = (f32[8,64,128]{2,1,0:T(8,128)S(1)}, f32[8,64,128]{2,1,0:T(8,128)S(1)}, u32[]{:S(2)}, u32[]{:S(2)}) collective-permute-start(f32[8,64,128]{2,1,0:T(8,128)S(1)} %multiply_add_fusion.7), channel_id=1, source_target_pairs={{16,0},{32,16},{48,32},{64,48},{80,64},{96,80},{112,96},{128,112},... | collective-permute-start | bytes 786440 | tf_op jit(solution)/shard_map/while/body/eval_jaxpr/ppermute | solution.py:16
  400.8 8.9 %collective-permute-start.1 = (f32[8,64,128]{2,1,0:T(8,128)S(1)}, f32[8,64,128]{2,1,0:T(8,128)S(1)}, u32[]{:S(2)}, u32[]{:S(2)}) collective-permute-start(f32[8,64,128]{2,1,0:T(8,128)S(1)} %multiply_add_fusion.7), channel_id=1, source_target_pairs={{16,0},{32,16},{48,32},{64,48},{80,64},{96,80},{112,96},{128,112},... | collective-permute-start | bytes 786440 | tf_op jit(solution)/shard_map/while/body/eval_jaxpr/ppermute | solution.py:16
  512.4 149.7 %collective-permute-start.4 = (f32[3,512]{0,1:T(8,128)S(1)}, f32[3,512]{0,1:T(8,128)S(1)}, u32[]{:S(2)}, u32[]{:S(2)}) collective-permute-start(f32[3,512]{0,1:T(8,128)S(1)} %slice.175), channel_id=1, source_target_pairs={{16,0},{32,16},{48,32},{64,48},{80,64},{96,80},{112,96},{128,112},... | collective-permute-start | bytes 18440 | tf_op jit(solution)/shard_map/ppermute | solution.py:16
  (48 other events, 1221.0 us)
Sparse Core Ops, SparseCore 0:
  508.5 93.7 reduce-scatter.1
where the time goes:
time: 679 us; the launch traced here: 673 us
  blocking collectives  206 us (30%)
  waiting for transfers between devices  159 us (23%)
  starting transfers between devices  115 us (17%)
  local copies, waits for them, and re-layouts  93.2 us (14%)
  other arithmetic  42.8 us (6%)
  matrix products  41.9 us (6%)
  between operations  14.8 us (2%)
    ppermute x34, waiting for transfers between devices, passed_along(): return lax.ppermute(block, axis, route)  159 us
    ppermute x34, starting transfers between devices, passed_along(): return lax.ppermute(block, axis, route)  115 us
    psum x1, blocking collectives, local(): grad_convbc = lax.psum(grad_convbc_part, ('ctx', 'head'))  80.8 us
    psum x1, blocking collectives, local(): lax.psum((grad_alog_part, grad_skip_part, grad_convx_part, grad_gain_part...  62.7 us
    psum x2, blocking collectives, local(): lax.psum((jnp.sum(gated_out * gated_out, axis=1), jnp.sum(scaled_grad * g...  62.4 us
    dynamic_update_slice x8, local copies, waits for them, and re-layouts, local(): lax.map(forward_block, (x_blocks, b_blocks, c_blocks, d_blocks, cum_block...  48.2 us
  transfers between devices with their start and end apart: 35, of which 31 were waited for; matrix products, arithmetic and copies ran while one was open for 4% of the time, Pallas kernels for 0%

commit v1 on v0

--- a/solution.py
+++ b/solution.py
@@ -223,7 +223,7 @@
     grad_alog, grad_dskip, grad_convx, grad_gain = lax.psum(
         (grad_alog_part, grad_skip_part, grad_convx_part, grad_gain_part), "ctx"
     )
-    grad_convbc = lax.psum(grad_convbc_part, ("ctx", "head"))
+    grad_convbc = jnp.sum(lax.all_gather(grad_convbc_part, ("ctx", "head")), axis=0)
     return (
         y_out,
         grad_x,

time: 679 us -> 650 us (0.957)
  blocking collectives: 206 us -> 125 us
  waiting for transfers between devices: 159 us -> 209 us
    psum x1 -> x0, blocking collectives: 80.8 us -> none  [local(): grad_convbc = lax.psum(grad_convbc_part, ('ctx', 'head'))]
    all_gather x0 -> x1, waiting for transfers between devices: none -> 29.8 us  [local(): lax.all_gather(grad_convbc_part, ('ctx', 'head'))]
    reduce_scatter x1, waiting for transfers between devices: 0.01 us -> 19.7 us  [local(): shares = lax.psum_scatter(bc_back, 'head', scatter_dimension=0, tiled=True)]
  transfers between devices with their start and end apart: 35 -> 36, of which waited for: 31 -> 33; matrix products, arithmetic and copies ran while one was open for 4% -> 3% of each run, Pallas kernels for 0% -> 0%
where the time goes in v1:
time: 650 us; the launch traced here: 644 us
  waiting for transfers between devices  209 us (32%)
  blocking collectives  125 us (19%)
  starting transfers between devices  115 us (18%)
  local copies, waits for them, and re-layouts  92.6 us (14%)
  other arithmetic  43.1 us (7%)
  matrix products  41.9 us (6%)
  between operations  16.2 us (2%)
    ppermute x34, waiting for transfers between devices, passed_along(): return lax.ppermute(block, axis, route)  160 us
    ppermute x34, starting transfers between devices, passed_along(): return lax.ppermute(block, axis, route)  115 us
    psum x1, blocking collectives, local(): lax.psum((grad_alog_part, grad_skip_part, grad_convx_part, grad_gain_part...  62.8 us
    psum x2, blocking collectives, local(): lax.psum((jnp.sum(gated_out * gated_out, axis=1), jnp.sum(scaled_grad * g...  62.4 us
    dynamic_update_slice x8, local copies, waits for them, and re-layouts, local(): lax.map(forward_block, (x_blocks, b_blocks, c_blocks, d_blocks, cum_block...  48.2 us
    all_gather x1, waiting for transfers between devices, local(): lax.all_gather(grad_convbc_part, ('ctx', 'head'))  29.8 us
    reduce_scatter x1, waiting for transfers between devices, local(): shares = lax.psum_scatter(bc_back, 'head', scatter_dimension=0, tiled=True)  19.7 us
  transfers between devices with their start and end apart: 36, of which 33 were waited for; matrix products, arithmetic and copies ran while one was open for 3% of the time, Pallas kernels for 0%

profile of v1, /device:TPU:1, one launch (start us, length us, event | category | flops | bytes accessed | tf_op | source)
XLA Modules:
  0.0 643.9 jit_solution(3535077294561585186)
XLA Ops:
  9.0 4.9 collective-permute-start.2
  36.4 116.3 %while.77 = (s32[]{:T(128)}, f32[8,64,128]{2,1,0:T(8,128)S(1)}, f32[8]{0:T(128)S(1)}, f32[8,64,128]{2,1,0:T(8,128)S(1)}, s32[]{:T(128)}) while((s32[]{:T(128)}, f32[8,64,128]{2,1,0:T(8,128)S(1)}, f32[8]{0:T(128)S(1)}, f32[8,64,128]{2,1,0:T(8,128)S(1)}, s32[]{:T(128)}) %tuple.173), condition=%wide.region_7.8_spmd, body=%wide.region_6.7_spmd.sunk | while | flops 131074 | bytes 1835141 | solution.py:112
  51.7 4.4 collective-permute-start
  154.3 36.2 %while.78 = (s32[]{:T(128)}, f32[2,256,8,64]{1,0,3,2:T(2,128)}, f32[2,256,8,64]{1,3,2,0:T(8,128)}, f32[2,256,128]{2,1,0:T(8,128)S(1)}, f32[2,256,128]{2,1,0:T(8,...) while((s32[]{:T(128)}, f32[2,256,8,64]{1,0,3,2:T(2,128)}, ...), condition=%wide.region_9.10_spmd, body=%wide.region_8.9_spmd.sunk | while | flops 707592192 | bytes 5580925 | solution.py:126
  160.8 11.5 %dynamic_update_slice.48 = f32[2,256,8,64]{1,0,3,2:T(2,128)} dynamic-update-slice(f32[2,256,8,64]{1,0,3,2:T(2,128)} %get-tuple-element.953, f32[1,256,8,64]{1,0,3,2:T(1,128)S(1)} %copy.219, s32[]{:T(128)S(6)} %copy.255, s32[]{:T(128)} %constant.125.clone.1..sunk, s32[]{:T(128)} %constant.125.clone.1..sunk, s32[]{:T(128)} %constant.125.clone.1..sunk) | dynamic-update-slice | bytes 1048580 | tf_op jit(solution)/shard_map/while/body/jit(dynamic_update_index_in_dim)/dynamic_update_slice | solution.py:126
  178.9 11.5 %dynamic_update_slice.48 = f32[2,256,8,64]{1,0,3,2:T(2,128)} dynamic-update-slice(f32[2,256,8,64]{1,0,3,2:T(2,128)} %get-tuple-element.953, f32[1,256,8,64]{1,0,3,2:T(1,128)S(1)} %copy.219, s32[]{:T(128)S(6)} %copy.255, s32[]{:T(128)} %constant.125.clone.1..sunk, s32[]{:T(128)} %constant.125.clone.1..sunk, s32[]{:T(128)} %constant.125.clone.1..sunk) | dynamic-update-slice | bytes 1048580 | tf_op jit(solution)/shard_map/while/body/jit(dynamic_update_index_in_dim)/dynamic_update_slice | solution.py:126
  192.8 33.5 %psum.42 = f32[512]{0:T(512)S(1)} all-reduce(f32[512]{0:T(512)S(1)} %get-tuple-element.601), channel_id=1, replica_groups=mesh['ctx'=16,'head'=16] {'head'}, use_global_device_ids=true, to_apply=%region_11.12 | all-reduce | flops 512 | bytes 4096 | tf_op jit(solution)/shard_map/psum | solution.py:136
  228.4 28.9 %psum.43 = f32[512]{0:T(512)S(1)} all-reduce(f32[512]{0:T(512)S(1)} %get-tuple-element.496), channel_id=1, replica_groups=mesh['ctx'=16,'head'=16] {'head'}, use_global_device_ids=true, to_apply=%region_13.14 | all-reduce | flops 512 | bytes 4096 | tf_op jit(solution)/shard_map/psum | solution.py:136
  257.3 4.5 multiply_reduce_fusion.3
  264.3 146.2 %while.79 = (s32[]{:T(128)}, f32[8,64,128]{2,1,0:T(8,128)S(1)}, f32[8]{0:T(128)S(1)}, f32[8,64,128]{2,1,0:T(8,128)S(1)}, s32[]{:T(128)}) while((s32[]{:T(128)}, f32[8,64,128]{2,1,0:T(8,128)S(1)}, f32[8]{0:T(128)S(1)}, f32[8,64,128]{2,1,0:T(8,128)S(1)}, s32[]{:T(128)}) %tuple.197), condition=%wide.region_16.17_spmd, body=%wide.region_15.16_spmd.sunk | while | flops 131074 | bytes 1835141 | solution.py:158
  264.4 11.7 %collective-permute-start.1 = (f32[8,64,128]{2,1,0:T(8,128)S(1)}, f32[8,64,128]{2,1,0:T(8,128)S(1)}, u32[]{:S(2)}, u32[]{:S(2)}) collective-permute-start(f32[8,64,128]{2,1,0:T(8,128)S(1)} %multiply_add_fusion.7), channel_id=1, source_target_pairs={{16,0},{32,16},{48,32},{64,48},{80,64},{96,80},{112,96},{128,112},... | collective-permute-start | bytes 786440 | tf_op jit(solution)/shard_map/while/body/eval_jaxpr/ppermute | solution.py:16
  276.1 10.6 %collective-permute-done.1 = f32[8,64,128]{2,1,0:T(8,128)S(1)} collective-permute-done((f32[8,64,128]{2,1,0:T(8,128)S(1)}, f32[8,64,128]{2,1,0:T(8,128)S(1)}, u32[]{:S(2)}, u32[]{:S(2)}) %collective-permute-start.1) | collective-permute-done | bytes 262176 | tf_op jit(solution)/shard_map/while/body/eval_jaxpr/ppermute | solution.py:16
  288.7 5.8 collective-permute-done.1
  296.5 5.8 collective-permute-done.1
  304.3 5.8 collective-permute-done.1
  312.1 7.8 %collective-permute-done.1 = f32[8,64,128]{2,1,0:T(8,128)S(1)} collective-permute-done((f32[8,64,128]{2,1,0:T(8,128)S(1)}, f32[8,64,128]{2,1,0:T(8,128)S(1)}, u32[]{:S(2)}, u32[]{:S(2)}) %collective-permute-start.1) | collective-permute-done | bytes 262176 | tf_op jit(solution)/shard_map/while/body/eval_jaxpr/ppermute | solution.py:16
  321.9 5.8 collective-permute-done.1
  329.7 8.8 %collective-permute-done.1 = f32[8,64,128]{2,1,0:T(8,128)S(1)} collective-permute-done((f32[8,64,128]{2,1,0:T(8,128)S(1)}, f32[8,64,128]{2,1,0:T(8,128)S(1)}, u32[]{:S(2)}, u32[]{:S(2)}) %collective-permute-start.1) | collective-permute-done | bytes 262176 | tf_op jit(solution)/shard_map/while/body/eval_jaxpr/ppermute | solution.py:16
  340.5 7.0 %collective-permute-done.1 = f32[8,64,128]{2,1,0:T(8,128)S(1)} collective-permute-done((f32[8,64,128]{2,1,0:T(8,128)S(1)}, f32[8,64,128]{2,1,0:T(8,128)S(1)}, u32[]{:S(2)}, u32[]{:S(2)}) %collective-permute-start.1) | collective-permute-done | bytes 262176 | tf_op jit(solution)/shard_map/while/body/eval_jaxpr/ppermute | solution.py:16
  349.5 7.0 %collective-permute-done.1 = f32[8,64,128]{2,1,0:T(8,128)S(1)} collective-permute-done((f32[8,64,128]{2,1,0:T(8,128)S(1)}, f32[8,64,128]{2,1,0:T(8,128)S(1)}, u32[]{:S(2)}, u32[]{:S(2)}) %collective-permute-start.1) | collective-permute-done | bytes 262176 | tf_op jit(solution)/shard_map/while/body/eval_jaxpr/ppermute | solution.py:16
  358.5 7.0 %collective-permute-done.1 = f32[8,64,128]{2,1,0:T(8,128)S(1)} collective-permute-done((f32[8,64,128]{2,1,0:T(8,128)S(1)}, f32[8,64,128]{2,1,0:T(8,128)S(1)}, u32[]{:S(2)}, u32[]{:S(2)}) %collective-permute-start.1) | collective-permute-done | bytes 262176 | tf_op jit(solution)/shard_map/while/body/eval_jaxpr/ppermute | solution.py:16
  367.5 7.0 %collective-permute-done.1 = f32[8,64,128]{2,1,0:T(8,128)S(1)} collective-permute-done((f32[8,64,128]{2,1,0:T(8,128)S(1)}, f32[8,64,128]{2,1,0:T(8,128)S(1)}, u32[]{:S(2)}, u32[]{:S(2)}) %collective-permute-start.1) | collective-permute-done | bytes 262176 | tf_op jit(solution)/shard_map/while/body/eval_jaxpr/ppermute | solution.py:16
  376.5 7.0 %collective-permute-done.1 = f32[8,64,128]{2,1,0:T(8,128)S(1)} collective-permute-done((f32[8,64,128]{2,1,0:T(8,128)S(1)}, f32[8,64,128]{2,1,0:T(8,128)S(1)}, u32[]{:S(2)}, u32[]{:S(2)}) %collective-permute-start.1) | collective-permute-done | bytes 262176 | tf_op jit(solution)/shard_map/while/body/eval_jaxpr/ppermute | solution.py:16
  385.5 7.0 %collective-permute-done.1 = f32[8,64,128]{2,1,0:T(8,128)S(1)} collective-permute-done((f32[8,64,128]{2,1,0:T(8,128)S(1)}, f32[8,64,128]{2,1,0:T(8,128)S(1)}, u32[]{:S(2)}, u32[]{:S(2)}) %collective-permute-start.1) | collective-permute-done | bytes 262176 | tf_op jit(solution)/shard_map/while/body/eval_jaxpr/ppermute | solution.py:16
  394.5 7.0 %collective-permute-done.1 = f32[8,64,128]{2,1,0:T(8,128)S(1)} collective-permute-done((f32[8,64,128]{2,1,0:T(8,128)S(1)}, f32[8,64,128]{2,1,0:T(8,128)S(1)}, u32[]{:S(2)}, u32[]{:S(2)}) %collective-permute-start.1) | collective-permute-done | bytes 262176 | tf_op jit(solution)/shard_map/while/body/eval_jaxpr/ppermute | solution.py:16
  403.5 7.0 %collective-permute-done.1 = f32[8,64,128]{2,1,0:T(8,128)S(1)} collective-permute-done((f32[8,64,128]{2,1,0:T(8,128)S(1)}, f32[8,64,128]{2,1,0:T(8,128)S(1)}, u32[]{:S(2)}, u32[]{:S(2)}) %collective-permute-start.1) | collective-permute-done | bytes 262176 | tf_op jit(solution)/shard_map/while/body/eval_jaxpr/ppermute | solution.py:16
  412.2 87.2 %while.81 = (s32[]{:T(128)}, f32[2,256,8,64]{1,0,3,2:T(2,128)}, f32[2,256,128]{2,1,0:T(8,128)}, f32[2,256,128]{2,1,0:T(8,128)}, f32[2,256,8]{1,2,0:T(8,128)}, /*...) while((s32[]{:T(128)}, f32[2,256,8,64]{1,0,3,2:T(2,128)}, ...), condition=%wide.region_30.31_spmd, body=%wide.region_19.30_spmd.sunk | while | flops 1921460224 | bytes 14728557 | solution.py:197
  444.3 11.5 %dynamic_update_slice.53 = f32[2,256,8,64]{1,0,3,2:T(2,128)} dynamic-update-slice(f32[2,256,8,64]{1,0,3,2:T(2,128)} %get-tuple-element.1024, f32[1,256,8,64]{1,0,3,2:T(1,128)S(1)} %copy.225, s32[]{:T(128)S(6)} %copy.280, s32[]{:T(128)} %constant.125.clone.1..sunk.1, s32[]{:T(128)} %constant.125.clone.1..sunk.1, s32[]{:T(128)} %constant.125.clone.1..sunk.1) | dynamic-update-slice | bytes 1048580 | tf_op jit(solution)/shard_map/while/body/jit(dynamic_update_index_in_dim)/dynamic_update_slice | solution.py:126
  487.9 11.5 %dynamic_update_slice.53 = f32[2,256,8,64]{1,0,3,2:T(2,128)} dynamic-update-slice(f32[2,256,8,64]{1,0,3,2:T(2,128)} %get-tuple-element.1024, f32[1,256,8,64]{1,0,3,2:T(1,128)S(1)} %copy.225, s32[]{:T(128)S(6)} %copy.280, s32[]{:T(128)} %constant.125.clone.1..sunk.1, s32[]{:T(128)} %constant.125.clone.1..sunk.1, s32[]{:T(128)} %constant.125.clone.1..sunk.1) | dynamic-update-slice | bytes 1048580 | tf_op jit(solution)/shard_map/while/body/jit(dynamic_update_index_in_dim)/dynamic_update_slice | solution.py:126
  516.2 62.8 %all-reduce = (f32[8]{0:T(128)}, f32[8]{0:T(128)}, f32[4,512]{1,0:T(4,128)}, f32[512]{0:T(512)}) all-reduce(f32[8]{0:T(128)S(1)} %negate_multiply_fusion, f32[8]{0:T(128)S(1)} %reduce_sum.234, f32[4,512]{1,0:T(4,128)S(1)} %pad_maximum_fusion.5, f32[512]{0:T(512)S(1)} %copy-done.42), channel_id=1, replica_groups=mesh['ctx'=16,'head'=16] {'ctx'}, use_global_device_ids=true, to_apply=%region_33.34 | all-reduce | flops 2576 | bytes 20608 | tf_op jit(solution)/shard_map/psum | solution.py:223
  583.5 19.7 %reduce-scatter.2.cloned.1.call-done = f32[32,256]{1,0:T(8,128)} async-done(((f32[512,256]{1,0:T(8,128)}), f32[32,256]{1,0:T(8,128)}) %reduce-scatter.2.cloned.1.call-update) | async-done | bytes 32784 | tf_op jit(solution)/shard_map/reduce_scatter | solution.py:218
  604.6 29.8 %all-gather.4.cloned.1.call-done = f32[256,4,256]{2,1,0:T(4,128)} async-done(((f32[1,4,256]{2,1,0:T(4,128)}), f32[256,4,256]{2,1,0:T(4,128)}) %all-gather.4.cloned.1.call-update) | async-done | bytes 1048592 | tf_op jit(solution)/shard_map/all_gather | solution.py:226
  (347 shorter events, 275.3 us)
Async XLA Ops:
  8.0 595.2 %reduce-scatter.2.cloned.1.call-start = ((), (), s32[]{:S(2)}) async-start(), calls=%async_computation.1 | async-start | bytes 557056 | tf_op jit(solution)/shard_map/reduce_scatter | solution.py:218
  9.0 20.1 %collective-permute-start.2 = (bf16[3,512]{0,1:T(8,128)(2,1)S(1)}, bf16[3,512]{0,1:T(8,128)(2,1)S(1)}, u32[]{:S(2)}, u32[]{:S(2)}) collective-permute-start(bf16[3,512]{0,1:T(8,128)(2,1)S(1)} %copy.135), channel_id=1, source_target_pairs={{0,16},{16,32},{32,48},{48,64},{64,80},{80,96},{96,112},{112,128},... | collective-permute-start | bytes 9224 | tf_op jit(solution)/shard_map/ppermute | solution.py:16
  15.8 12.9 %collective-permute-start.3 = (bf16[3,256]{1,0:T(4,128)(2,1)S(1)}, bf16[3,256]{1,0:T(4,128)(2,1)S(1)}, u32[]{:S(2)}, u32[]{:S(2)}) collective-permute-start(bf16[3,256]{1,0:T(4,128)(2,1)S(1)} %slice.165), channel_id=1, source_target_pairs={{0,16},{16,32},{32,48},{48,64},{64,80},{80,96},{96,112},{112,128},... | collective-permute-start | bytes 4616 | tf_op jit(solution)/shard_map/ppermute | solution.py:16
  43.9 7.7 %collective-permute-start = (f32[8,64,128]{2,1,0:T(8,128)S(1)}, f32[8,64,128]{2,1,0:T(8,128)S(1)}, u32[]{:S(2)}, u32[]{:S(2)}) collective-permute-start(f32[8,64,128]{2,1,0:T(8,128)S(1)} %multiply_add_fusion.6), channel_id=1, source_target_pairs={{0,16},{16,32},{32,48},{48,64},{64,80},{80,96},{96,112},{112,128},... | collective-permute-start | bytes 786440 | tf_op jit(solution)/shard_map/while/body/eval_jaxpr/ppermute | solution.py:16
  51.7 7.7 %collective-permute-start = (f32[8,64,128]{2,1,0:T(8,128)S(1)}, f32[8,64,128]{2,1,0:T(8,128)S(1)}, u32[]{:S(2)}, u32[]{:S(2)}) collective-permute-start(f32[8,64,128]{2,1,0:T(8,128)S(1)} %multiply_add_fusion.6), channel_id=1, source_target_pairs={{0,16},{16,32},{32,48},{48,64},{64,80},{80,96},{96,112},{112,128},... | collective-permute-start | bytes 786440 | tf_op jit(solution)/shard_map/while/body/eval_jaxpr/ppermute | solution.py:16
  59.4 7.7 %collective-permute-start = (f32[8,64,128]{2,1,0:T(8,128)S(1)}, f32[8,64,128]{2,1,0:T(8,128)S(1)}, u32[]{:S(2)}, u32[]{:S(2)}) collective-permute-start(f32[8,64,128]{2,1,0:T(8,128)S(1)} %multiply_add_fusion.6), channel_id=1, source_target_pairs={{0,16},{16,32},{32,48},{48,64},{64,80},{80,96},{96,112},{112,128},... | collective-permute-start | bytes 786440 | tf_op jit(solution)/shard_map/while/body/eval_jaxpr/ppermute | solution.py:16
  67.2 7.7 %collective-permute-start = (f32[8,64,128]{2,1,0:T(8,128)S(1)}, f32[8,64,128]{2,1,0:T(8,128)S(1)}, u32[]{:S(2)}, u32[]{:S(2)}) collective-permute-start(f32[8,64,128]{2,1,0:T(8,128)S(1)} %multiply_add_fusion.6), channel_id=1, source_target_pairs={{0,16},{16,32},{32,48},{48,64},{64,80},{80,96},{96,112},{112,128},... | collective-permute-start | bytes 786440 | tf_op jit(solution)/shard_map/while/body/eval_jaxpr/ppermute | solution.py:16
  75.0 7.7 %collective-permute-start = (f32[8,64,128]{2,1,0:T(8,128)S(1)}, f32[8,64,128]{2,1,0:T(8,128)S(1)}, u32[]{:S(2)}, u32[]{:S(2)}) collective-permute-start(f32[8,64,128]{2,1,0:T(8,128)S(1)} %multiply_add_fusion.6), channel_id=1, source_target_pairs={{0,16},{16,32},{32,48},{48,64},{64,80},{80,96},{96,112},{112,128},... | collective-permute-start | bytes 786440 | tf_op jit(solution)/shard_map/while/body/eval_jaxpr/ppermute | solution.py:16
  82.8 7.7 %collective-permute-start = (f32[8,64,128]{2,1,0:T(8,128)S(1)}, f32[8,64,128]{2,1,0:T(8,128)S(1)}, u32[]{:S(2)}, u32[]{:S(2)}) collective-permute-start(f32[8,64,128]{2,1,0:T(8,128)S(1)} %multiply_add_fusion.6), channel_id=1, source_target_pairs={{0,16},{16,32},{32,48},{48,64},{64,80},{80,96},{96,112},{112,128},... | collective-permute-start | bytes 786440 | tf_op jit(solution)/shard_map/while/body/eval_jaxpr/ppermute | solution.py:16
  90.6 7.7 %collective-permute-start = (f32[8,64,128]{2,1,0:T(8,128)S(1)}, f32[8,64,128]{2,1,0:T(8,128)S(1)}, u32[]{:S(2)}, u32[]{:S(2)}) collective-permute-start(f32[8,64,128]{2,1,0:T(8,128)S(1)} %multiply_add_fusion.6), channel_id=1, source_target_pairs={{0,16},{16,32},{32,48},{48,64},{64,80},{80,96},{96,112},{112,128},... | collective-permute-start | bytes 786440 | tf_op jit(solution)/shard_map/while/body/eval_jaxpr/ppermute | solution.py:16
  98.4 7.7 %collective-permute-start = (f32[8,64,128]{2,1,0:T(8,128)S(1)}, f32[8,64,128]{2,1,0:T(8,128)S(1)}, u32[]{:S(2)}, u32[]{:S(2)}) collective-permute-start(f32[8,64,128]{2,1,0:T(8,128)S(1)} %multiply_add_fusion.6), channel_id=1, source_target_pairs={{0,16},{16,32},{32,48},{48,64},{64,80},{80,96},{96,112},{112,128},... | collective-permute-start | bytes 786440 | tf_op jit(solution)/shard_map/while/body/eval_jaxpr/ppermute | solution.py:16
  106.2 7.7 %collective-permute-start = (f32[8,64,128]{2,1,0:T(8,128)S(1)}, f32[8,64,128]{2,1,0:T(8,128)S(1)}, u32[]{:S(2)}, u32[]{:S(2)}) collective-permute-start(f32[8,64,128]{2,1,0:T(8,128)S(1)} %multiply_add_fusion.6), channel_id=1, source_target_pairs={{0,16},{16,32},{32,48},{48,64},{64,80},{80,96},{96,112},{112,128},... | collective-permute-start | bytes 786440 | tf_op jit(solution)/shard_map/while/body/eval_jaxpr/ppermute | solution.py:16
  113.9 7.7 %collective-permute-start = (f32[8,64,128]{2,1,0:T(8,128)S(1)}, f32[8,64,128]{2,1,0:T(8,128)S(1)}, u32[]{:S(2)}, u32[]{:S(2)}) collective-permute-start(f32[8,64,128]{2,1,0:T(8,128)S(1)} %multiply_add_fusion.6), channel_id=1, source_target_pairs={{0,16},{16,32},{32,48},{48,64},{64,80},{80,96},{96,112},{112,128},... | collective-permute-start | bytes 786440 | tf_op jit(solution)/shard_map/while/body/eval_jaxpr/ppermute | solution.py:16
  121.7 7.7 %collective-permute-start = (f32[8,64,128]{2,1,0:T(8,128)S(1)}, f32[8,64,128]{2,1,0:T(8,128)S(1)}, u32[]{:S(2)}, u32[]{:S(2)}) collective-permute-start(f32[8,64,128]{2,1,0:T(8,128)S(1)} %multiply_add_fusion.6), channel_id=1, source_target_pairs={{0,16},{16,32},{32,48},{48,64},{64,80},{80,96},{96,112},{112,128},... | collective-permute-start | bytes 786440 | tf_op jit(solution)/shard_map/while/body/eval_jaxpr/ppermute | solution.py:16
  129.5 7.7 %collective-permute-start = (f32[8,64,128]{2,1,0:T(8,128)S(1)}, f32[8,64,128]{2,1,0:T(8,128)S(1)}, u32[]{:S(2)}, u32[]{:S(2)}) collective-permute-start(f32[8,64,128]{2,1,0:T(8,128)S(1)} %multiply_add_fusion.6), channel_id=1, source_target_pairs={{0,16},{16,32},{32,48},{48,64},{64,80},{80,96},{96,112},{112,128},... | collective-permute-start | bytes 786440 | tf_op jit(solution)/shard_map/while/body/eval_jaxpr/ppermute | solution.py:16
  137.3 7.7 %collective-permute-start = (f32[8,64,128]{2,1,0:T(8,128)S(1)}, f32[8,64,128]{2,1,0:T(8,128)S(1)}, u32[]{:S(2)}, u32[]{:S(2)}) collective-permute-start(f32[8,64,128]{2,1,0:T(8,128)S(1)} %multiply_add_fusion.6), channel_id=1, source_target_pairs={{0,16},{16,32},{32,48},{48,64},{64,80},{80,96},{96,112},{112,128},... | collective-permute-start | bytes 786440 | tf_op jit(solution)/shard_map/while/body/eval_jaxpr/ppermute | solution.py:16
  145.1 7.7 %collective-permute-start = (f32[8,64,128]{2,1,0:T(8,128)S(1)}, f32[8,64,128]{2,1,0:T(8,128)S(1)}, u32[]{:S(2)}, u32[]{:S(2)}) collective-permute-start(f32[8,64,128]{2,1,0:T(8,128)S(1)} %multiply_add_fusion.6), channel_id=1, source_target_pairs={{0,16},{16,32},{32,48},{48,64},{64,80},{80,96},{96,112},{112,128},... | collective-permute-start | bytes 786440 | tf_op jit(solution)/shard_map/while/body/eval_jaxpr/ppermute | solution.py:16
  264.4 22.3 %collective-permute-start.1 = (f32[8,64,128]{2,1,0:T(8,128)S(1)}, f32[8,64,128]{2,1,0:T(8,128)S(1)}, u32[]{:S(2)}, u32[]{:S(2)}) collective-permute-start(f32[8,64,128]{2,1,0:T(8,128)S(1)} %multiply_add_fusion.7), channel_id=1, source_target_pairs={{16,0},{32,16},{48,32},{64,48},{80,64},{96,80},{112,96},{128,112},... | collective-permute-start | bytes 786440 | tf_op jit(solution)/shard_map/while/body/eval_jaxpr/ppermute | solution.py:16
  286.8 7.7 %collective-permute-start.1 = (f32[8,64,128]{2,1,0:T(8,128)S(1)}, f32[8,64,128]{2,1,0:T(8,128)S(1)}, u32[]{:S(2)}, u32[]{:S(2)}) collective-permute-start(f32[8,64,128]{2,1,0:T(8,128)S(1)} %multiply_add_fusion.7), channel_id=1, source_target_pairs={{16,0},{32,16},{48,32},{64,48},{80,64},{96,80},{112,96},{128,112},... | collective-permute-start | bytes 786440 | tf_op jit(solution)/shard_map/while/body/eval_jaxpr/ppermute | solution.py:16
  294.6 7.7 %collective-permute-start.1 = (f32[8,64,128]{2,1,0:T(8,128)S(1)}, f32[8,64,128]{2,1,0:T(8,128)S(1)}, u32[]{:S(2)}, u32[]{:S(2)}) collective-permute-start(f32[8,64,128]{2,1,0:T(8,128)S(1)} %multiply_add_fusion.7), channel_id=1, source_target_pairs={{16,0},{32,16},{48,32},{64,48},{80,64},{96,80},{112,96},{128,112},... | collective-permute-start | bytes 786440 | tf_op jit(solution)/shard_map/while/body/eval_jaxpr/ppermute | solution.py:16
  310.1 9.7 %collective-permute-start.1 = (f32[8,64,128]{2,1,0:T(8,128)S(1)}, f32[8,64,128]{2,1,0:T(8,128)S(1)}, u32[]{:S(2)}, u32[]{:S(2)}) collective-permute-start(f32[8,64,128]{2,1,0:T(8,128)S(1)} %multiply_add_fusion.7), channel_id=1, source_target_pairs={{16,0},{32,16},{48,32},{64,48},{80,64},{96,80},{112,96},{128,112},... | collective-permute-start | bytes 786440 | tf_op jit(solution)/shard_map/while/body/eval_jaxpr/ppermute | solution.py:16
  327.8 10.7 %collective-permute-start.1 = (f32[8,64,128]{2,1,0:T(8,128)S(1)}, f32[8,64,128]{2,1,0:T(8,128)S(1)}, u32[]{:S(2)}, u32[]{:S(2)}) collective-permute-start(f32[8,64,128]{2,1,0:T(8,128)S(1)} %multiply_add_fusion.7), channel_id=1, source_target_pairs={{16,0},{32,16},{48,32},{64,48},{80,64},{96,80},{112,96},{128,112},... | collective-permute-start | bytes 786440 | tf_op jit(solution)/shard_map/while/body/eval_jaxpr/ppermute | solution.py:16
  338.6 8.9 %collective-permute-start.1 = (f32[8,64,128]{2,1,0:T(8,128)S(1)}, f32[8,64,128]{2,1,0:T(8,128)S(1)}, u32[]{:S(2)}, u32[]{:S(2)}) collective-permute-start(f32[8,64,128]{2,1,0:T(8,128)S(1)} %multiply_add_fusion.7), channel_id=1, source_target_pairs={{16,0},{32,16},{48,32},{64,48},{80,64},{96,80},{112,96},{128,112},... | collective-permute-start | bytes 786440 | tf_op jit(solution)/shard_map/while/body/eval_jaxpr/ppermute | solution.py:16
  347.6 8.9 %collective-permute-start.1 = (f32[8,64,128]{2,1,0:T(8,128)S(1)}, f32[8,64,128]{2,1,0:T(8,128)S(1)}, u32[]{:S(2)}, u32[]{:S(2)}) collective-permute-start(f32[8,64,128]{2,1,0:T(8,128)S(1)} %multiply_add_fusion.7), channel_id=1, source_target_pairs={{16,0},{32,16},{48,32},{64,48},{80,64},{96,80},{112,96},{128,112},... | collective-permute-start | bytes 786440 | tf_op jit(solution)/shard_map/while/body/eval_jaxpr/ppermute | solution.py:16
  356.6 8.9 %collective-permute-start.1 = (f32[8,64,128]{2,1,0:T(8,128)S(1)}, f32[8,64,128]{2,1,0:T(8,128)S(1)}, u32[]{:S(2)}, u32[]{:S(2)}) collective-permute-start(f32[8,64,128]{2,1,0:T(8,128)S(1)} %multiply_add_fusion.7), channel_id=1, source_target_pairs={{16,0},{32,16},{48,32},{64,48},{80,64},{96,80},{112,96},{128,112},... | collective-permute-start | bytes 786440 | tf_op jit(solution)/shard_map/while/body/eval_jaxpr/ppermute | solution.py:16
  365.6 8.9 %collective-permute-start.1 = (f32[8,64,128]{2,1,0:T(8,128)S(1)}, f32[8,64,128]{2,1,0:T(8,128)S(1)}, u32[]{:S(2)}, u32[]{:S(2)}) collective-permute-start(f32[8,64,128]{2,1,0:T(8,128)S(1)} %multiply_add_fusion.7), channel_id=1, source_target_pairs={{16,0},{32,16},{48,32},{64,48},{80,64},{96,80},{112,96},{128,112},... | collective-permute-start | bytes 786440 | tf_op jit(solution)/shard_map/while/body/eval_jaxpr/ppermute | solution.py:16
  374.6 8.9 %collective-permute-start.1 = (f32[8,64,128]{2,1,0:T(8,128)S(1)}, f32[8,64,128]{2,1,0:T(8,128)S(1)}, u32[]{:S(2)}, u32[]{:S(2)}) collective-permute-start(f32[8,64,128]{2,1,0:T(8,128)S(1)} %multiply_add_fusion.7), channel_id=1, source_target_pairs={{16,0},{32,16},{48,32},{64,48},{80,64},{96,80},{112,96},{128,112},... | collective-permute-start | bytes 786440 | tf_op jit(solution)/shard_map/while/body/eval_jaxpr/ppermute | solution.py:16
  383.6 8.9 %collective-permute-start.1 = (f32[8,64,128]{2,1,0:T(8,128)S(1)}, f32[8,64,128]{2,1,0:T(8,128)S(1)}, u32[]{:S(2)}, u32[]{:S(2)}) collective-permute-start(f32[8,64,128]{2,1,0:T(8,128)S(1)} %multiply_add_fusion.7), channel_id=1, source_target_pairs={{16,0},{32,16},{48,32},{64,48},{80,64},{96,80},{112,96},{128,112},... | collective-permute-start | bytes 786440 | tf_op jit(solution)/shard_map/while/body/eval_jaxpr/ppermute | solution.py:16
  392.6 8.9 %collective-permute-start.1 = (f32[8,64,128]{2,1,0:T(8,128)S(1)}, f32[8,64,128]{2,1,0:T(8,128)S(1)}, u32[]{:S(2)}, u32[]{:S(2)}) collective-permute-start(f32[8,64,128]{2,1,0:T(8,128)S(1)} %multiply_add_fusion.7), channel_id=1, source_target_pairs={{16,0},{32,16},{48,32},{64,48},{80,64},{96,80},{112,96},{128,112},... | collective-permute-start | bytes 786440 | tf_op jit(solution)/shard_map/while/body/eval_jaxpr/ppermute | solution.py:16
  401.6 8.9 %collective-permute-start.1 = (f32[8,64,128]{2,1,0:T(8,128)S(1)}, f32[8,64,128]{2,1,0:T(8,128)S(1)}, u32[]{:S(2)}, u32[]{:S(2)}) collective-permute-start(f32[8,64,128]{2,1,0:T(8,128)S(1)} %multiply_add_fusion.7), channel_id=1, source_target_pairs={{16,0},{32,16},{48,32},{64,48},{80,64},{96,80},{112,96},{128,112},... | collective-permute-start | bytes 786440 | tf_op jit(solution)/shard_map/while/body/eval_jaxpr/ppermute | solution.py:16
  509.4 125.0 %all-gather.4.cloned.1.call-start = ((), (), s32[]{:S(2)}) async-start(), calls=%async_computation.2 | async-start | bytes 1052672 | tf_op jit(solution)/shard_map/all_gather | solution.py:226
  513.1 67.9 %collective-permute-start.4 = (f32[3,512]{0,1:T(8,128)S(1)}, f32[3,512]{0,1:T(8,128)S(1)}, u32[]{:S(2)}, u32[]{:S(2)}) collective-permute-start(f32[3,512]{0,1:T(8,128)S(1)} %slice.175), channel_id=1, source_target_pairs={{16,0},{32,16},{48,32},{64,48},{80,64},{96,80},{112,96},{128,112},... | collective-permute-start | bytes 18440 | tf_op jit(solution)/shard_map/ppermute | solution.py:16
  (51 other events, 971.0 us)
Sparse Core Ops, SparseCore 0:
  509.5 93.7 reduce-scatter.1
Sparse Core Ops, SparseCore 1:
  514.1 120.2 all-gather.3
